TPU v7x, 256 devices: a whole 4x4x8 slice. The times are simulated.
256 devices in a mesh: req: 32 (over x, y, core), kv: 8 (over z).
Axes of the slice: x: 4, y: 4, z: 8, core: 2. Of those that a mesh axis runs over, the one named last changes fastest.
Arguments:
- hidden: bfloat16 [512, 1536], P('req'), may hold values from -6 to 6
- norm_gain: float32 [1536], replicated, may hold values from 0.5 to 1.5
- w_qkv: bfloat16 [1536, 3072], P(None, 'kv'), may hold values from -0.15625 to 0.15625
- w_out: bfloat16 [1536, 1536], P(None, 'kv'), may hold values from -0.15625 to 0.15625
- cache_pages: bfloat16 [6144, 2, 8, 96, 128], P('req', None, 'kv'), may hold values from -340 to 340
- lengths: int32 [512], P('req'), may hold values from 1 to 16384, as said below
- page_table: int32 [512, 128], P('req'), may hold values from 0 to 191, as said below
- occupant: int32 [512], replicated, may hold values from 0 to 511, each once
Outputs:
- mixed: bfloat16 [512, 1536], P('req', 'kv')
Inputs may be any that keep to these rules, and one draw needn't show every extreme that they name: `occupant`: every request is served at exactly one slot. Slot s holds ceil(lengths[s] / 128) pages; on every index of req the pages of its 16 slots fit its pool of 192, some pool is full, and some request has 16384 tokens. `page_table`: the first ceil(lengths[s] / 128) entries of slot s are pages of its own pool that no other slot of that pool uses; later entries are arbitrary pages of the pool.
All inputs are finite; a program needn't handle non-finite values.
Results may differ from a plain program's by a relative error of at most 0.0043.
Values may be sent and summed in bfloat16 or wider, within the bound.
No kernel may reach another device: no remote copies, remote signals or barrier semaphores. Data moves between devices by JAX's collectives and lax.ppermute only.
A program may use at most 64 MiB of HBM per device.

v0:
```python
import math
import jax
import jax.numpy as jnp
from jax import lax
from jax.sharding import PartitionSpec as P

HD = 96
PAGE = 128
MAXP = 128
GROUP = 2


def per_device(hidden, norm_gain, w_qkv, w_out, cache_pages, lengths, page_table, occupant):
    slot_count = hidden.shape[0]
    pool_size = cache_pages.shape[0]
    kv_local = cache_pages.shape[2]
    first_slot = lax.axis_index("req") * slot_count
    hidden_wide = hidden.astype(jnp.float32)
    normed = (
        hidden_wide
        * lax.rsqrt(jnp.mean(hidden_wide * hidden_wide, axis=1, keepdims=True) + 1e-05)
        * norm_gain
    ).astype(jnp.bfloat16)
    served = lax.dynamic_slice_in_dim(occupant, first_slot, slot_count)
    own_rows = jnp.dot(normed, w_qkv, preferred_element_type=jnp.float32).astype(jnp.bfloat16)
    every_row = lax.all_gather(own_rows, "req", axis=0, tiled=True)
    slot_rows = jnp.take(every_row, served, axis=0)
    slot_rows = slot_rows.reshape(slot_count, kv_local, GROUP + 2, HD)
    queries = slot_rows[:, :, :GROUP]
    own_key = slot_rows[:, :, GROUP]
    own_value = slot_rows[:, :, GROUP + 1]
    score_scale = 1.0 / math.sqrt(HD)
    pages_used = (lengths + PAGE - 1) // PAGE
    live_page = jnp.arange(MAXP, dtype=jnp.int32)[None, :] < pages_used[:, None]
    matches = (
        (page_table[:, :, None] == jnp.arange(pool_size, dtype=jnp.int32)[None, None, :])
        & live_page[:, :, None]
    ).astype(jnp.int32)
    owner_table = jnp.sum(matches, axis=1)
    slot_ids = jnp.arange(slot_count, dtype=jnp.int32)
    page_owner = jnp.sum(owner_table * slot_ids[:, None], axis=0)
    page_rank = jnp.sum(matches * jnp.arange(MAXP, dtype=jnp.int32)[None, :, None], axis=(0, 1))
    page_limit = jnp.sum(owner_table * lengths[:, None], axis=0)
    offsets = page_rank[:, None] * PAGE + jnp.arange(PAGE, dtype=jnp.int32)[None, :]
    token_live = offsets < page_limit[:, None]
    page_queries = jnp.take(queries, page_owner, axis=0)
    scores = (
        jnp.einsum(
            "pgjd,pgdt->pgjt", page_queries, cache_pages[:, 0], preferred_element_type=jnp.float32
        )
        * score_scale
    )
    scores = jnp.where(token_live[:, None, None, :], scores, -jnp.inf)
    page_max = jnp.max(scores, axis=-1)
    own_score = (
        jnp.sum(queries.astype(jnp.float32) * own_key.astype(jnp.float32)[:, :, None, :], axis=-1)
        * score_scale
    )
    owner_mask = owner_table > 0
    slot_max = jnp.max(jnp.where(owner_mask[:, :, None, None], page_max[None], -jnp.inf), axis=1)
    slot_max = jnp.maximum(slot_max, own_score)
    weights = jnp.exp(scores - jnp.take(slot_max, page_owner, axis=0)[..., None])
    rounded = weights.astype(jnp.bfloat16)
    page_total = jnp.sum(weights, axis=-1)
    page_numerator = jnp.einsum(
        "pgjt,pgdt->pgjd", rounded, cache_pages[:, 1], preferred_element_type=jnp.float32
    )
    own_weight = jnp.exp(own_score - slot_max)
    own_rounded = lax.optimization_barrier(own_weight.astype(jnp.bfloat16)).astype(jnp.float32)
    owner_float = owner_table.astype(jnp.float32)
    denominator = (
        jnp.einsum("sp,pgj->sgj", owner_float, page_total, precision=lax.Precision.HIGHEST)
        + own_weight
    )
    numerator = jnp.einsum(
        "sp,pgjd->sgjd", owner_float, page_numerator, precision=lax.Precision.HIGHEST
    )
    numerator = numerator + own_rounded[..., None] * own_value.astype(jnp.float32)[:, :, None, :]
    context = (numerator / denominator[..., None]).astype(jnp.bfloat16).reshape(slot_count, -1)
    gathered = lax.all_gather(context, "req", axis=0, tiled=True)
    wanted = first_slot + slot_ids
    selector = (occupant[None, :] == wanted[:, None]).astype(jnp.bfloat16)
    attended = jnp.dot(selector, gathered, preferred_element_type=jnp.float32).astype(jnp.bfloat16)
    partial_value = lax.dot_general(
        attended, w_out, (((1,), (1,)), ((), ())), preferred_element_type=jnp.float32
    )
    summed = lax.psum_scatter(partial_value, "kv", scatter_dimension=1, tiled=True)
    col_share = summed.shape[1]
    residual = lax.dynamic_slice_in_dim(hidden_wide, lax.axis_index("kv") * col_share, col_share, 1)
    return (residual + summed).astype(jnp.bfloat16)


def solution(mesh):
    return jax.shard_map(
        per_device,
        mesh=mesh,
        in_specs=(
            P("req", None),
            P(),
            P(None, "kv"),
            P(None, "kv"),
            P("req", None, "kv", None, None),
            P("req"),
            P("req", None),
            P(),
        ),
        out_specs=P("req", "kv"),
        check_vma=False,
    )
```

profile of v0, /device:TPU:2, one launch (start us, length us, event | category | flops | bytes accessed | tf_op | source)
XLA Modules:
  0.0 121.7 jit_solution(13815415741669483195)
XLA Ops:
  6.6 0.9 compare_and_fusion
  7.4 0.9 multiply_reduce_fusion
  8.4 1.1 convolution_convert_fusion
  9.5 24.9 %all_gather.6 = bf16[512,384]{1,0:T(8,128)(2,1)S(1)} all-gather(bf16[16,384]{1,0:T(8,128)(2,1)S(1)} %convolution_convert_fusion), channel_id=1, replica_groups=mesh['req'=32,'kv'=8] {'req'}, dimensions={0}, use_global_device_ids=true | all-gather | bytes 405504 | tf_op jit(solution)/shard_map/all_gather | solution.py:26
  34.4 0.6 gather_fusion
  35.1 0.1 broadcast_select_fusion.3
  35.3 1.0 select_reduce_fusion
  36.3 0.1 multiply_reduce_fusion.2
  36.4 0.1 multiply_reduce_fusion.1
  36.6 0.8 gather_fusion.1
  37.5 0.1 add_compare_fusion
  37.6 3.8 %fusion.38 = (f32[192,2]{1,0:T(8,128)S(1)}, f32[192,2,128]{2,1,0:T(2,128)S(1)}) fusion(bf16[192,2,1,96,128]{4,3,2,1,0:T(8,128)(2,1)} %param.12, bf16[192,2,96]{2,1,0:T(2,128)(2,1)S(1)} %gather_fusion.1, pred[192]{0:T(512)(128)(4,1)S(1)} %compare_and_fusion.1, pred[192,128]{1,0:T(8,128)(4,1)S(1)} %add_compare_fusion), kind=kOutput, calls=%fused_computation.76 | convolution fusion | flops 9621120 | bytes 5015232 | tf_op jit(solution)/shard_map/pgjd,pgdt->pgjt/dot_general | solution.py:48
  41.5 0.1 select_reduce_fusion.1
  41.7 0.7 gather_fusion.2
  42.4 0.1 broadcast_select_fusion.2
  42.5 0.5 fusion.16
  43.1 5.0 %fusion = f32[192,2,96]{2,1,0:T(2,128)S(1)} fusion(bf16[192,2,1,96,128]{4,3,2,1,0:T(8,128)(2,1)} %param.12, f32[192,2,128]{2,1,0:T(2,128)S(1)} %get-tuple-element.16, f32[192,2]{1,0:T(8,128)S(1)} %broadcast_select_fusion.2), kind=kOutput, calls=%fused_computation.3 | convolution fusion | flops 9535488 | bytes 5064192 | tf_op jit(solution)/shard_map/pgjt,pgdt->pgjd/dot_general | solution.py:65
  48.1 0.3 convolution_add_fusion.1
  48.4 0.3 fusion.11
  48.7 23.1 %all_gather.7 = bf16[512,192]{1,0:T(8,128)(2,1)S(1)} all-gather(bf16[16,192]{1,0:T(8,128)(2,1)S(1)} %reshape.245), channel_id=1, replica_groups=mesh['req'=32,'kv'=8] {'req'}, dimensions={0}, use_global_device_ids=true | all-gather | bytes 202752 | tf_op jit(solution)/shard_map/all_gather | solution.py:80
  71.8 1.5 %convolution_bitcast_fusion = f32[1536,16]{1,0:T(8,128)} fusion(bf16[1536,192]{0,1:T(8,128)(2,1)S(1)} %copy-done.1, bf16[512,192]{1,0:T(8,128)(2,1)S(1)} %all_gather.7, s32[512]{0:T(512)S(1)} %copy-done.4, s32[16]{0:T(128)S(1)} %iota_add_fusion), kind=kOutput, calls=%fused_computation.9 | convolution fusion | flops 12594176 | bytes 886848
  73.3 39.9 %reduce-scatter.4.cloned.1.call-done = f32[192,16]{1,0:T(8,128)} async-done(((f32[1536,16]{1,0:T(8,128)}), f32[192,16]{1,0:T(8,128)}) %reduce-scatter.4.cloned.1.call-update) | async-done | bytes 12304
  113.2 0.9 copy.35
  114.2 0.7 add_convert_fusion
  (35 shorter events, 0.6 us)
Async XLA Ops:
  6.5 1.8 %copy-start = (bf16[1536,384]{1,0:T(8,128)(2,1)S(1)}, bf16[1536,384]{1,0:T(8,128)(2,1)}, u32[]{:S(2)}) copy-start(bf16[1536,384]{1,0:T(8,128)(2,1)} %param.10) | copy-start | bytes 3538948
  6.5 28.7 %copy-start.5 = (s32[16]{0:T(128)S(1)}, s32[16]{0:T(128)}, u32[]{:S(2)}) copy-start(s32[16]{0:T(128)} %param.13) | copy-start | bytes 196
  6.5 28.8 %copy-start.3 = (s32[16,128]{1,0:T(8,128)S(1)}, s32[16,128]{1,0:T(8,128)}, u32[]{:S(2)}) copy-start(s32[16,128]{1,0:T(8,128)} %param.14) | copy-start | bytes 24580
  6.5 106.7 %reduce-scatter.4.cloned.1.call-start = ((), (), s32[]{:S(2)}) async-start(), calls=%async_computation.1 | async-start | bytes 884736
  43.1 28.8 %copy-start.1 = (bf16[1536,192]{0,1:T(8,128)(2,1)S(1)}, bf16[1536,192]{0,1:T(8,128)(2,1)}, u32[]{:S(2)}) copy-start(bf16[1536,192]{0,1:T(8,128)(2,1)} %param.11) | copy-start | bytes 1769476
  43.1 28.7 %copy-start.4 = (s32[512]{0:T(512)S(1)}, s32[512]{0:T(512)}, u32[]{:S(2)}) copy-start(s32[512]{0:T(512)} %param.15) | copy-start | bytes 6148
  48.1 25.2 %copy-start.2 = (bf16[16,1536]{1,0:T(8,128)(2,1)S(1)}, bf16[16,1536]{1,0:T(8,128)(2,1)}, u32[]{:S(2)}) copy-start(bf16[16,1536]{1,0:T(8,128)(2,1)} %param.8) | copy-start | bytes 147460
Sparse Core Ops, SparseCore 0:
  73.4 39.7 reduce-scatter.3
where the time goes:
time: 122 us
  blocking collectives  47.9 us (39%)
  waiting for transfers between devices  39.9 us (33%)
  between operations  13.6 us (11%)
  matrix products  12 us (10%)
  other arithmetic  4.73 us (4%)
  local copies, waits for them, and re-layouts  3.55 us (3%)
    unnamed x2, waiting for transfers between devices  39.9 us
    all_gather x1, blocking collectives, per_device(): every_row = lax.all_gather(own_rows, 'req', axis=0, tiled=True)  24.9 us
    all_gather x1, blocking collectives, per_device(): gathered = lax.all_gather(context, 'req', axis=0, tiled=True)  23.1 us
    dot_general x1, matrix products, per_device(): jnp.einsum('pgjt,pgdt->pgjd', rounded, cache_pages[:, 1], preferred_eleme...  5.01 us
    dot_general x1, matrix products, per_device(): jnp.einsum('pgjd,pgdt->pgjt', page_queries, cache_pages[:, 0], preferred_...  3.85 us
  transfers between devices with their start and end apart: 1, of which 1 were waited for; matrix products, arithmetic and copies ran while one was open for 0% of the time, Pallas kernels for 0%

commit v1 on v0

--- a/solution.py
+++ b/solution.py
@@ -8,6 +8,19 @@
 PAGE = 128
 MAXP = 128
 GROUP = 2
+
+
+def _close_types(matrix, peer_axis):
+    later = jnp.concatenate(
+        lax.all_to_all(
+            jnp.stack([matrix for _ in range(lax.axis_size(peer_axis))]),
+            axis_name=peer_axis,
+            split_axis=0,
+            concat_axis=0,
+        ),
+        axis=0,
+    )
+    return later
 
 
 def per_device(hidden, norm_gain, w_qkv, w_out, cache_pages, lengths, page_table, occupant):
@@ -77,7 +90,7 @@
     )
     numerator = numerator + own_rounded[..., None] * own_value.astype(jnp.float32)[:, :, None, :]
     context = (numerator / denominator[..., None]).astype(jnp.bfloat16).reshape(slot_count, -1)
-    gathered = lax.all_gather(context, "req", axis=0, tiled=True)
+    gathered = _close_types(context, "req")
     wanted = first_slot + slot_ids
     selector = (occupant[None, :] == wanted[:, None]).astype(jnp.bfloat16)
     attended = jnp.dot(selector, gathered, preferred_element_type=jnp.float32).astype(jnp.bfloat16)

time: 122 us -> 112 us (0.918)
  blocking collectives: 47.9 us -> 24.9 us
  waiting for transfers between devices: 39.9 us -> 46.3 us
  starting transfers between devices: 0.01 us -> 5.76 us
    all_gather x1 -> x0, blocking collectives: 23.1 us -> none  [per_device(): gathered = lax.all_gather(context, 'req', axis=0, tiled=True)]
    all_to_all x0 -> x1, waiting for transfers between devices: none -> 7.63 us  [_close_types(): lax.all_to_all(jnp.stack([matrix for _ in range(lax.axis_size(peer_axis))...]
    all_to_all x0 -> x1, starting transfers between devices: none -> 5.72 us  [_close_types(): lax.all_to_all(jnp.stack([matrix for _ in range(lax.axis_size(peer_axis))...]
  transfers between devices with their start and end apart: 1 -> 2, of which waited for: 1 -> 2; matrix products, arithmetic and copies ran while one was open for 0% -> 0% of each run, Pallas kernels for 0% -> 0%
where the time goes in v1:
time: 112 us
  waiting for transfers between devices  46.3 us (41%)
  blocking collectives  24.9 us (22%)
  between operations  13.6 us (12%)
  matrix products  12 us (11%)
  starting transfers between devices  5.76 us (5%)
  other arithmetic  4.73 us (4%)
  local copies, waits for them, and re-layouts  4.25 us (4%)
    unnamed x2, waiting for transfers between devices  38.7 us
    all_gather x1, blocking collectives, per_device(): every_row = lax.all_gather(own_rows, 'req', axis=0, tiled=True)  24.9 us
    all_to_all x1, waiting for transfers between devices, _close_types(): lax.all_to_all(jnp.stack([matrix for _ in range(lax.axis_size(peer_axis))...  7.63 us
    all_to_all x1, starting transfers between devices, _close_types(): lax.all_to_all(jnp.stack([matrix for _ in range(lax.axis_size(peer_axis))...  5.72 us
    dot_general x1, matrix products, per_device(): jnp.einsum('pgjt,pgdt->pgjd', rounded, cache_pages[:, 1], preferred_eleme...  4.95 us
    dot_general x1, matrix products, per_device(): jnp.einsum('pgjd,pgdt->pgjt', page_queries, cache_pages[:, 0], preferred_...  3.85 us
  transfers between devices with their start and end apart: 2, of which 2 were waited for; matrix products, arithmetic and copies ran while one was open for 0% of the time, Pallas kernels for 0%

profile of v1, /device:TPU:2, one launch (start us, length us, event | category | flops | bytes accessed | tf_op | source)
XLA Modules:
  0.0 111.5 jit_solution(7787076767201274260)
XLA Ops:
  6.5 0.9 compare_and_fusion
  7.4 0.9 multiply_reduce_fusion
  8.3 1.1 %convolution_convert_fusion = bf16[16,384]{1,0:T(8,128)(2,1)S(1)} fusion(bf16[1536,384]{1,0:T(8,128)(2,1)S(1)} %copy-done, f32[1536]{0:T(1024)} %param.9, f32[16]{0:T(128)S(1)} %add_rsqrt_fusion, bf16[16,1536]{1,0:T(8,128)(2,1)} %param.8), kind=kOutput, calls=%fused_computation.15 | convolution fusion | flops 18978816 | bytes 1247296 | tf_op jit(solution)/shard_map/dot_general | solution.py:38
  9.5 24.9 %all_gather.3 = bf16[512,384]{1,0:T(8,128)(2,1)S(1)} all-gather(bf16[16,384]{1,0:T(8,128)(2,1)S(1)} %convolution_convert_fusion), channel_id=1, replica_groups=mesh['req'=32,'kv'=8] {'req'}, dimensions={0}, use_global_device_ids=true | all-gather | bytes 405504 | tf_op jit(solution)/shard_map/all_gather | solution.py:39
  34.4 0.6 gather_fusion
  35.0 0.1 broadcast_select_fusion.3
  35.3 1.0 select_reduce_fusion
  36.4 0.1 multiply_reduce_fusion.1
  36.6 0.8 gather_fusion.1
  37.4 0.1 add_compare_fusion
  37.6 3.9 %fusion.38 = (f32[192,2]{1,0:T(8,128)S(1)}, f32[192,2,128]{2,1,0:T(2,128)S(1)}) fusion(bf16[192,2,1,96,128]{4,3,2,1,0:T(8,128)(2,1)} %param.12, bf16[192,2,96]{2,1,0:T(2,128)(2,1)S(1)} %gather_fusion.1, pred[192]{0:T(512)(128)(4,1)S(1)} %compare_and_fusion.1, pred[192,128]{1,0:T(8,128)(4,1)S(1)} %add_compare_fusion), kind=kOutput, calls=%fused_computation.76 | convolution fusion | flops 9621120 | bytes 5015232 | tf_op jit(solution)/shard_map/pgjd,pgdt->pgjt/dot_general | solution.py:61
  41.5 0.1 select_reduce_fusion.1
  41.7 0.7 gather_fusion.2
  42.5 0.5 fusion.16
  43.1 5.0 %fusion = f32[192,2,96]{2,1,0:T(2,128)S(1)} fusion(bf16[192,2,1,96,128]{4,3,2,1,0:T(8,128)(2,1)} %param.12, f32[192,2,128]{2,1,0:T(2,128)S(1)} %get-tuple-element.16, f32[192,2]{1,0:T(8,128)S(1)} %broadcast_select_fusion.2), kind=kOutput, calls=%fused_computation.3 | convolution fusion | flops 9535488 | bytes 5064192 | tf_op jit(solution)/shard_map/pgjt,pgdt->pgjd/dot_general | solution.py:78
  48.0 0.3 convolution_add_fusion.1
  48.3 0.3 fusion.11
  48.7 0.7 stack.3
  49.4 5.7 %all-to-all-start = ((bf16[32,16,192]{2,1,0:T(8,128)(2,1)}), bf16[32,16,192]{2,1,0:T(8,128)(2,1)S(1)}, u32[]{:S(2)}, u32[]{:S(2)}) async-start(bf16[32,16,192]{2,1,0:T(8,128)(2,1)} %stack.3), calls=%async_computation | async-start | bytes 524288 | tf_op jit(solution)/shard_map/all_to_all | solution.py:15
  55.2 7.6 %all-to-all-done = bf16[32,16,192]{2,1,0:T(8,128)(2,1)S(1)} async-done(((bf16[32,16,192]{2,1,0:T(8,128)(2,1)}), bf16[32,16,192]{2,1,0:T(8,128)(2,1)S(1)}, u32[]{:S(2)}, u32[]{:S(2)}) %all-to-all-start) | async-done | bytes 196640 | tf_op jit(solution)/shard_map/all_to_all | solution.py:15
  62.8 1.5 %convolution_bitcast_fusion = f32[1536,16]{1,0:T(8,128)} fusion(bf16[1536,192]{0,1:T(8,128)(2,1)S(1)} %copy-done.1, bf16[512,192]{1,0:T(8,128)(2,1)S(1)} %bitcast.55, s32[512]{0:T(512)S(1)} %copy-done.4, s32[16]{0:T(128)S(1)} %iota_add_fusion), kind=kOutput, calls=%fused_computation.9 | convolution fusion | flops 12594176 | bytes 886848
  64.4 38.7 %reduce-scatter.4.cloned.1.call-done = f32[192,16]{1,0:T(8,128)} async-done(((f32[1536,16]{1,0:T(8,128)}), f32[192,16]{1,0:T(8,128)}) %reduce-scatter.4.cloned.1.call-update) | async-done | bytes 12304
  103.0 0.9 copy.35
  104.0 0.7 add_convert_fusion
  (37 shorter events, 0.9 us)
Async XLA Ops:
  6.5 1.8 %copy-start = (bf16[1536,384]{1,0:T(8,128)(2,1)S(1)}, bf16[1536,384]{1,0:T(8,128)(2,1)}, u32[]{:S(2)}) copy-start(bf16[1536,384]{1,0:T(8,128)(2,1)} %param.10) | copy-start | bytes 3538948
  6.5 28.6 %copy-start.5 = (s32[16]{0:T(128)S(1)}, s32[16]{0:T(128)}, u32[]{:S(2)}) copy-start(s32[16]{0:T(128)} %param.13) | copy-start | bytes 196
  6.5 28.7 %copy-start.3 = (s32[16,128]{1,0:T(8,128)S(1)}, s32[16,128]{1,0:T(8,128)}, u32[]{:S(2)}) copy-start(s32[16,128]{1,0:T(8,128)} %param.14) | copy-start | bytes 24580
  43.0 19.8 %copy-start.4 = (s32[512]{0:T(512)S(1)}, s32[512]{0:T(512)}, u32[]{:S(2)}) copy-start(s32[512]{0:T(512)} %param.15) | copy-start | bytes 6148
  48.0 14.8 %copy-start.1 = (bf16[1536,192]{0,1:T(8,128)(2,1)S(1)}, bf16[1536,192]{0,1:T(8,128)(2,1)}, u32[]{:S(2)}) copy-start(bf16[1536,192]{0,1:T(8,128)(2,1)} %param.11) | copy-start | bytes 1769476
  48.7 15.7 %copy-start.2 = (bf16[16,1536]{1,0:T(8,128)(2,1)S(1)}, bf16[16,1536]{1,0:T(8,128)(2,1)}, u32[]{:S(2)}) copy-start(bf16[16,1536]{1,0:T(8,128)(2,1)} %param.8) | copy-start | bytes 147460
  49.4 13.4 %all-to-all-start = ((bf16[32,16,192]{2,1,0:T(8,128)(2,1)}), bf16[32,16,192]{2,1,0:T(8,128)(2,1)S(1)}, u32[]{:S(2)}, u32[]{:S(2)}) async-start(bf16[32,16,192]{2,1,0:T(8,128)(2,1)} %stack.3), calls=%async_computation | async-start | bytes 524288 | tf_op jit(solution)/shard_map/all_to_all | solution.py:15
  55.1 47.9 %reduce-scatter.4.cloned.1.call-start = ((), (), s32[]{:S(2)}) async-start(), calls=%async_computation.2 | async-start | bytes 884736
Sparse Core Ops, SparseCore 0:
  64.4 38.5 reduce-scatter.3
